TPU v7x, 256 devices: a whole 4x4x8 slice. The times are simulated.
256 devices in a mesh: pair: 32 (over z, x_lo, core), grp: 8 (over y, x_hi).
Axes of the slice: x: 4 (x_hi: 2, x_lo: 2; x = x_hi * 2 + x_lo), y: 4, z: 8, core: 2. Of those that a mesh axis runs over, the one named last changes fastest.
Arguments:
- amplitudes: float32 [8, 224, 2048], P('grp', 'pair'), may hold values from -6 to 6
- integrals: float32 [2048, 65536], P('grp', 'pair'), may hold values from -0.375 to 0.375
- owner_blocks: int32 [16], replicated, may hold values from 0 to 15, each once
- occ_pairs: int32 [8, 2, 224], P('grp'), may hold values from 0 to 63, as said below
- vir_pairs: int32 [2, 65536], replicated, may hold values from 0 to 511, as said below
- occ_energy: float32 [64], replicated, may hold values from -1.5 to -0.5
- vir_energy: float32 [512], replicated, may hold values from 0.2 to 1.5
Outputs:
- ladder: float32 [8, 224, 65536], P('grp', 'pair')
Inputs may be any that keep to these rules, and one draw needn't show every extreme that they name: `occ_pairs`: each column is a pair i<j; no pair occurs twice. `vir_pairs`: each column is a pair a<b; no pair occurs twice. `owner_blocks`: a permutation.
All inputs are finite; a program needn't handle non-finite values.
Results may differ from a plain program's by a relative error of at most 0.000071.
Values sent between devices are 32-bit elements; how exact they have to be, the bound alone decides.
No kernel may reach another device: no remote copies, remote signals or barrier semaphores. Data moves between devices by JAX's collectives and lax.ppermute only.
A program may use at most 64 MiB of HBM per device.

v0:
```python
import jax
import jax.numpy as jnp
import numpy as np
from jax import lax
from jax.sharding import Mesh, PartitionSpec as P

N_CHUNK = 4


def pair_energies(energy, pairs):
    return jnp.take(energy, pairs[0]) + jnp.take(energy, pairs[1])


def on_device(amplitudes, integrals, owner_blocks, occ_pairs, vir_pairs, occ_energy, vir_energy):
    rows_l = amplitudes.shape[1]
    width = amplitudes.shape[2]
    block = integrals.shape[0]
    columns = integrals.shape[1]
    nblocks = owner_blocks.shape[0]
    sub = width // nblocks
    per_block = block // sub
    ny = lax.axis_size("gy")
    nx = lax.axis_size("gx")
    npair = lax.axis_size("pair")
    gx = lax.axis_index("gx")
    p = lax.axis_index("pair")

    def half_blocks(x):
        m = jnp.arange(ny * per_block, dtype=jnp.int32)
        b = (m // per_block * nx + x) * per_block + m % per_block
        return jnp.take(owner_blocks, b)

    tau = amplitudes[0].reshape(rows_l, nblocks, sub)

    def select(x):
        return jnp.take(tau, half_blocks(x), axis=1).reshape(rows_l, -1)

    mine = select(gx)
    other = select(1 - gx)
    swap = [(0, 1), (1, 0)]
    got = lax.ppermute(other, "gx", swap)
    both = jnp.where(gx == 0, jnp.stack([mine, got]), jnp.stack([got, mine]))
    spread = jnp.broadcast_to(both[None], (npair,) + both.shape)
    t_all = lax.all_to_all(spread, "pair", 0, 0, tiled=True)
    lhs = t_all.reshape(npair * nx * rows_l, -1)
    occ_sum = pair_energies(occ_energy, occ_pairs[0]).reshape(npair, rows_l)
    vir_local = lax.dynamic_slice_in_dim(vir_pairs, p * columns, columns, 1)
    vir_sum = pair_energies(vir_energy, vir_local)
    w = columns // N_CHUNK
    outs = []
    for c in range(N_CHUNK):
        piece = lax.all_gather(integrals[:, c * w : (c + 1) * w], "gy", axis=0, tiled=True)
        part = jnp.dot(
            lhs, piece, precision=lax.Precision.HIGHEST, preferred_element_type=jnp.float32
        )
        part = part.reshape(npair, nx, rows_l, w)
        keep = lax.dynamic_index_in_dim(part, gx, 1, keepdims=False)
        send = lax.dynamic_index_in_dim(part, 1 - gx, 1, keepdims=False)
        work = keep + lax.ppermute(send, "gx", swap)
        payload = work / (occ_sum[:, :, None] - vir_sum[None, None, c * w : (c + 1) * w])
        outs.append(lax.all_to_all(payload, "pair", 0, 0, tiled=True))
    res = jnp.stack(outs, axis=2)
    res = jnp.transpose(res, (1, 0, 2, 3)).reshape(1, rows_l, npair * columns)
    return res


def solution(mesh):
    devs = np.asarray(mesh.devices)
    npair, ngrp = devs.shape
    nx = 2
    sub_mesh = Mesh(devs.reshape(npair, ngrp // nx, nx), ("pair", "gy", "gx"))
    g = ("gy", "gx")
    return jax.shard_map(
        on_device,
        mesh=sub_mesh,
        in_specs=(P(g, "pair", None), P(g, "pair"), P(), P(g, None, None), P(), P(), P()),
        out_specs=P(g, "pair", None),
        check_vma=False,
    )
```

profile of v0, /device:TPU:2, one launch (start us, length us, event | category | flops | bytes accessed | tf_op | source)
XLA Modules:
  0.0 309.0 jit_solution(17155572473532148239)
XLA Ops:
  6.5 3.0 fusion.20
  9.5 0.0 all-gather.9.cloned.1.call-update
  9.5 0.0 all-gather.11.cloned.1.call-start
  9.6 0.7 all-gather.11.cloned.1.call-update
  10.3 0.0 all-gather.7.cloned.1.call-start
  10.3 0.7 all-gather.7.cloned.1.call-update
  11.1 0.6 gather_fusion.2
  11.8 0.6 gather_fusion.3
  12.4 0.1 select_bitcast_fusion
  12.4 2.2 collective-permute-start
  14.6 0.6 gather_fusion
  15.3 0.6 gather_fusion.1
  15.9 0.1 select_bitcast_fusion.1
  15.9 2.0 collective-permute-done
  18.0 1.7 broadcast_in_dim.34
  19.7 10.2 %all-to-all-start = ((f32[32,2,7,1024]{3,1,2,0:T(2,128)}), f32[32,2,7,1024]{3,1,2,0:T(2,128)S(1)}, u32[]{:S(2)}, u32[]{:S(2)}) async-start(f32[32,2,7,1024]{3,1,2,0:T(2,128)} %broadcast_in_dim.34), calls=%async_computation | async-start | bytes 3670016 | tf_op jit(solution)/shard_map/all_to_all | solution.py:44
  29.9 0.0 all-gather.5.cloned.1.call-start
  29.9 0.5 all-gather.5.cloned.1.call-update
  30.5 1.9 gather_fusion.5
  32.4 2.0 gather_fusion.4
  34.5 0.9 constant_dynamic-slice_fusion
  35.4 10.6 %all-gather.9.cloned.1.call-done = f32[1024,512]{1,0:T(8,128)} async-done(((f32[256,512]{1,0:T(8,128)}), f32[1024,512]{1,0:T(8,128)}) %all-gather.9.cloned.1.call-update) | async-done | bytes 2097168 | tf_op jit(solution)/shard_map/all_gather | solution.py:52
  46.0 28.6 %all-to-all-done = f32[32,2,7,1024]{3,1,2,0:T(2,128)S(1)} async-done(((f32[32,2,7,1024]{3,1,2,0:T(2,128)}), f32[32,2,7,1024]{3,1,2,0:T(2,128)S(1)}, u32[]{:S(2)}, u32[]{:S(2)}) %all-to-all-start) | async-done | bytes 1835040 | tf_op jit(solution)/shard_map/all_to_all | solution.py:44
  74.6 5.2 %fusion.2 = f32[32,2,7,512]{3,0,2,1:T(8,128)S(1)} fusion(f32[1024,512]{1,0:T(8,128)} %all-gather.9.cloned.1.call-done, f32[32,2,7,1024]{3,1,2,0:T(2,128)S(1)} %all-to-all-done), kind=kOutput, calls=%fused_computation.11 | convolution fusion | flops 2818572288 | bytes 4849664 | tf_op jit(solution)/shard_map/dot_general | solution.py:53
  79.8 0.8 dynamic-slice_bitcast_fusion.1
  80.6 0.6 all-gather.11.cloned.1.call-done
  81.2 5.2 %fusion = f32[32,2,7,512]{3,0,2,1:T(8,128)S(1)} fusion(f32[1024,512]{1,0:T(8,128)} %all-gather.11.cloned.1.call-done, f32[32,2,7,1024]{3,1,2,0:T(2,128)S(1)} %all-to-all-done), kind=kOutput, calls=%fused_computation.9 | convolution fusion | flops 2818572288 | bytes 4849664 | tf_op jit(solution)/shard_map/dot_general | solution.py:53
  86.4 0.9 copy-done.3
  87.4 0.8 dynamic-slice_bitcast_fusion
  88.2 28.2 %all-gather.7.cloned.1.call-done = f32[1024,512]{1,0:T(8,128)} async-done(((f32[256,512]{1,0:T(8,128)}), f32[1024,512]{1,0:T(8,128)}) %all-gather.7.cloned.1.call-update) | async-done | bytes 2097168 | tf_op jit(solution)/shard_map/all_gather | solution.py:52
  116.4 5.2 %fusion.4 = f32[32,2,7,512]{3,0,2,1:T(8,128)S(1)} fusion(f32[1024,512]{1,0:T(8,128)} %all-gather.7.cloned.1.call-done, f32[32,2,7,1024]{3,1,2,0:T(2,128)S(1)} %all-to-all-done), kind=kOutput, calls=%fused_computation.13 | convolution fusion | flops 2818572288 | bytes 4849664 | tf_op jit(solution)/shard_map/dot_general | solution.py:53
  121.6 0.9 copy-done.5
  122.6 0.8 dynamic-slice_bitcast_fusion.2
  123.4 28.1 %all-gather.5.cloned.1.call-done = f32[1024,512]{1,0:T(8,128)} async-done(((f32[256,512]{1,0:T(8,128)}), f32[1024,512]{1,0:T(8,128)}) %all-gather.5.cloned.1.call-update) | async-done | bytes 2097168 | tf_op jit(solution)/shard_map/all_gather | solution.py:52
  151.5 5.4 %fusion.6 = f32[32,2,7,512]{3,0,2,1:T(8,128)S(1)} fusion(f32[1024,512]{1,0:T(8,128)} %all-gather.5.cloned.1.call-done, f32[32,2,7,1024]{3,1,2,0:T(2,128)S(1)} %all-to-all-done), kind=kOutput, calls=%fused_computation.15 | convolution fusion | flops 2818572288 | bytes 4849664 | tf_op jit(solution)/shard_map/dot_general | solution.py:53
  156.9 0.0 copy-start.7
  157.0 0.9 copy-done.7
  157.9 0.8 dynamic-slice_bitcast_fusion.3
  158.7 2.1 collective-permute-start.1
  160.7 1.4 collective-permute-start.2
  162.2 2.1 collective-permute-start.4
  164.3 1.4 collective-permute-start.3
  165.7 0.1 sub.31
  165.8 0.1 copy.44
  165.9 13.2 %gather_fusion.7 = f32[2048]{0:T(1024)S(1)} fusion(f32[512]{0:T(512)S(1)} %copy-done, s32[2048]{0:T(1024)S(1)} %fusion.17), kind=kCustom, calls=%fused_computation.7.clone | custom fusion | bytes 24576 | tf_op jit(solution)/shard_map/jit(_take)/gather | solution.py:11
  179.1 13.2 %gather_fusion.6 = f32[2048]{0:T(1024)S(1)} fusion(f32[512]{0:T(512)S(1)} %copy-done, s32[2048]{0:T(1024)S(1)} %fusion.16), kind=kCustom, calls=%fused_computation.3.clone | custom fusion | bytes 24576 | tf_op jit(solution)/shard_map/jit(_take)/gather | solution.py:11
  192.4 0.0 collective-permute-done.2
  192.4 1.1 collective-permute-done.4
  193.5 8.5 %collective-permute-done.3 = f32[32,7,512]{2,0,1:T(8,128)} collective-permute-done((f32[32,7,512]{2,0,1:T(8,128)}, f32[32,7,512]{2,0,1:T(8,128)}, u32[]{:S(2)}, u32[]{:S(2)}) %collective-permute-start.3) | collective-permute-done | bytes 458784 | tf_op jit(solution)/shard_map/ppermute | solution.py:59
  202.1 3.0 fusion.15
  205.1 1.1 copy.45
  206.1 8.6 %all-to-all-start.1 = ((f32[32,7,512]{2,1,0:T(8,128)}), f32[32,7,512]{2,1,0:T(8,128)S(1)}, u32[]{:S(2)}, u32[]{:S(2)}) async-start(f32[32,7,512]{2,1,0:T(8,128)} %copy.45), calls=%async_computation.1 | async-start | bytes 1048576 | tf_op jit(solution)/shard_map/all_to_all | solution.py:61
  214.8 1.1 copy.51
  215.8 16.6 %all-to-all-done.1 = f32[32,7,512]{2,1,0:T(8,128)S(1)} async-done(((f32[32,7,512]{2,1,0:T(8,128)}), f32[32,7,512]{2,1,0:T(8,128)S(1)}, u32[]{:S(2)}, u32[]{:S(2)}) %all-to-all-start.1) | async-done | bytes 458784 | tf_op jit(solution)/shard_map/all_to_all | solution.py:61
  232.4 3.8 %all-to-all-start.4 = ((f32[32,7,512]{2,1,0:T(8,128)}), f32[32,7,512]{2,1,0:T(8,128)S(1)}, u32[]{:S(2)}, u32[]{:S(2)}) async-start(f32[32,7,512]{2,1,0:T(8,128)} %copy.51), calls=%async_computation.4 | async-start | bytes 1048576 | tf_op jit(solution)/shard_map/all_to_all | solution.py:61
  236.2 1.1 copy.49
  237.3 16.7 %all-to-all-done.4 = f32[32,7,512]{2,1,0:T(8,128)S(1)} async-done(((f32[32,7,512]{2,1,0:T(8,128)}), f32[32,7,512]{2,1,0:T(8,128)S(1)}, u32[]{:S(2)}, u32[]{:S(2)}) %all-to-all-start.4) | async-done | bytes 458784 | tf_op jit(solution)/shard_map/all_to_all | solution.py:61
  254.0 4.1 %all-to-all-start.3 = ((f32[32,7,512]{2,1,0:T(8,128)}), f32[32,7,512]{2,1,0:T(8,128)S(1)}, u32[]{:S(2)}, u32[]{:S(2)}) async-start(f32[32,7,512]{2,1,0:T(8,128)} %copy.49), calls=%async_computation.3 | async-start | bytes 1048576 | tf_op jit(solution)/shard_map/all_to_all | solution.py:61
  258.1 0.3 copy.47
  258.4 17.5 %all-to-all-done.3 = f32[32,7,512]{2,1,0:T(8,128)S(1)} async-done(((f32[32,7,512]{2,1,0:T(8,128)}), f32[32,7,512]{2,1,0:T(8,128)S(1)}, u32[]{:S(2)}, u32[]{:S(2)}) %all-to-all-start.3) | async-done | bytes 458784 | tf_op jit(solution)/shard_map/all_to_all | solution.py:61
  275.9 21.0 %all_to_all.25 = f32[32,7,512]{2,1,0:T(8,128)S(1)} all-to-all(f32[32,7,512]{2,1,0:T(8,128)S(1)} %copy.47), channel_id=1, replica_groups=mesh['pair'=32,'gy'=4,'gx'=2] {'pair'}, dimensions={0} | all-to-all | bytes 917504 | tf_op jit(solution)/shard_map/all_to_all | solution.py:61
  296.8 0.3 maximum_bitcast_fusion
  297.1 1.2 copy.52
  298.3 4.2 %reshape.175 = f32[1,7,65536]{2,0,1:T(1,128)} reshape(f32[7,32,4,512]{3,2,1,0:T(4,128)S(1)} %copy.52) | data formatting | bytes 3670016 | tf_op jit(solution)/shard_map/reshape | solution.py:63
  (43 shorter events, 0.3 us)
Async XLA Ops:
  6.5 159.4 %copy-start = (f32[512]{0:T(512)S(1)}, f32[512]{0:T(512)}, u32[]{:S(2)}) copy-start(f32[512]{0:T(512)} %param.21) | copy-start | bytes 6148
  6.5 4.5 %copy-start.11 = (f32[1,7,2048]{2,0,1:T(1,128)S(1)}, f32[1,7,2048]{2,0,1:T(1,128)}, u32[]{:S(2)}) copy-start(f32[1,7,2048]{2,0,1:T(1,128)} %param.15) | copy-start | bytes 172036
  6.5 4.6 %copy-start.2 = (s32[16]{0:T(128)S(1)}, s32[16]{0:T(128)}, u32[]{:S(2)}) copy-start(s32[16]{0:T(128)} %param.17) | copy-start | bytes 196
  6.5 39.4 %all-gather.9.cloned.1.call-start = ((), (), s32[]{:S(2)}) async-start(), calls=%async_computation.7 | async-start | bytes 2621440 | tf_op jit(solution)/shard_map/all_gather | solution.py:52
  9.5 71.7 %all-gather.11.cloned.1.call-start = ((), (), s32[]{:S(2)}) async-start(), calls=%async_computation.8 | async-start | bytes 2621440 | tf_op jit(solution)/shard_map/all_gather | solution.py:52
  10.3 106.1 %all-gather.7.cloned.1.call-start = ((), (), s32[]{:S(2)}) async-start(), calls=%async_computation.6 | async-start | bytes 2621440 | tf_op jit(solution)/shard_map/all_gather | solution.py:52
  12.4 5.5 %collective-permute-start = (f32[7,1024]{1,0:T(8,128)S(1)}, f32[7,1024]{1,0:T(8,128)S(1)}, u32[]{:S(2)}, u32[]{:S(2)}) collective-permute-start(f32[7,1024]{1,0:T(8,128)S(1)} %select_bitcast_fusion), channel_id=1, source_target_pairs={{0,1},{1,0},{2,3},{3,2},{4,5},{5,4},{6,7},{7,6},{8,9},{9,8},{10,11... | collective-permute-start | bytes 86024 | tf_op jit(solution)/shard_map/ppermute | solution.py:41
  19.7 10.8 %copy-start.12 = (s32[1,2,224]{2,1,0:T(2,128)S(1)}, s32[1,2,224]{2,1,0:T(2,128)}, u32[]{:S(2)}) copy-start(s32[1,2,224]{2,1,0:T(2,128)} %param.18) | copy-start | bytes 5380
  19.7 10.9 %copy-start.1 = (f32[64]{0:T(128)S(1)}, f32[64]{0:T(128)}, u32[]{:S(2)}) copy-start(f32[64]{0:T(128)} %param.20) | copy-start | bytes 772
  19.7 54.9 %all-to-all-start = ((f32[32,2,7,1024]{3,1,2,0:T(2,128)}), f32[32,2,7,1024]{3,1,2,0:T(2,128)S(1)}, u32[]{:S(2)}, u32[]{:S(2)}) async-start(f32[32,2,7,1024]{3,1,2,0:T(2,128)} %broadcast_in_dim.34), calls=%async_computation | async-start | bytes 3670016 | tf_op jit(solution)/shard_map/all_to_all | solution.py:44
  29.9 121.6 %all-gather.5.cloned.1.call-start = ((), (), s32[]{:S(2)}) async-start(), calls=%async_computation.5 | async-start | bytes 2621440 | tf_op jit(solution)/shard_map/all_gather | solution.py:52
  86.4 1.0 copy-start.3
  121.6 0.9 copy-start.5
  156.9 0.9 copy-start.7
  158.7 33.7 %collective-permute-start.1 = (f32[32,7,512]{2,0,1:T(8,128)}, f32[32,7,512]{2,0,1:T(8,128)S(1)}, u32[]{:S(2)}, u32[]{:S(2)}) collective-permute-start(f32[32,7,512]{2,0,1:T(8,128)} %dynamic-slice_bitcast_fusion.3), channel_id=1, source_target_pairs={{0,1},{1,0},{2,3},{3,2},{4,5},{5,4},{6,7},{7,6},{8,9},{9,8},{10,11... | collective-permute-start | bytes 1376264 | tf_op jit(solution)/shard_map/ppermute | solution.py:59
  160.7 31.6 %collective-permute-start.2 = (f32[32,7,512]{2,0,1:T(8,128)}, f32[32,7,512]{2,0,1:T(8,128)}, u32[]{:S(2)}, u32[]{:S(2)}) collective-permute-start(f32[32,7,512]{2,0,1:T(8,128)} %dynamic-slice_bitcast_fusion.2), channel_id=1, source_target_pairs={{0,1},{1,0},{2,3},{3,2},{4,5},{5,4},{6,7},{7,6},{8,9},{9,8},{10,11... | collective-permute-start | bytes 1376264 | tf_op jit(solution)/shard_map/ppermute | solution.py:59
  162.2 31.3 %collective-permute-start.4 = (f32[32,7,512]{2,0,1:T(8,128)}, f32[32,7,512]{2,0,1:T(8,128)}, u32[]{:S(2)}, u32[]{:S(2)}) collective-permute-start(f32[32,7,512]{2,0,1:T(8,128)} %dynamic-slice_bitcast_fusion), channel_id=1, source_target_pairs={{0,1},{1,0},{2,3},{3,2},{4,5},{5,4},{6,7},{7,6},{8,9},{9,8},{10,11... | collective-permute-start | bytes 1376264 | tf_op jit(solution)/shard_map/ppermute | solution.py:59
  164.3 37.8 %collective-permute-start.3 = (f32[32,7,512]{2,0,1:T(8,128)}, f32[32,7,512]{2,0,1:T(8,128)}, u32[]{:S(2)}, u32[]{:S(2)}) collective-permute-start(f32[32,7,512]{2,0,1:T(8,128)} %dynamic-slice_bitcast_fusion.1), channel_id=1, source_target_pairs={{0,1},{1,0},{2,3},{3,2},{4,5},{5,4},{6,7},{7,6},{8,9},{9,8},{10,11... | collective-permute-start | bytes 1376264 | tf_op jit(solution)/shard_map/ppermute | solution.py:59
  179.1 23.0 %copy-start.4 = (f32[32,2,7,512]{3,0,2,1:T(8,128)S(1)}, f32[32,2,7,512]{3,0,2,1:T(8,128)}, u32[]{:S(2)}) copy-start(f32[32,2,7,512]{3,0,2,1:T(8,128)} %copy-done.3) | copy-start | bytes 2752516
  179.1 22.9 %copy-start.6 = (f32[32,2,7,512]{3,0,2,1:T(8,128)S(1)}, f32[32,2,7,512]{3,0,2,1:T(8,128)}, u32[]{:S(2)}) copy-start(f32[32,2,7,512]{3,0,2,1:T(8,128)} %copy-done.5) | copy-start | bytes 2752516
  192.4 9.7 %copy-start.10 = (f32[32,7,512]{2,0,1:T(8,128)}, f32[32,7,512]{2,0,1:T(8,128)S(1)}, u32[]{:S(2)}) copy-start(f32[32,7,512]{2,0,1:T(8,128)S(1)} %collective-permute-done.1) | copy-start | bytes 1376260
  205.1 9.7 %copy-start.9 = (f32[32,7,512]{2,0,1:T(8,128)S(1)}, f32[32,7,512]{2,0,1:T(8,128)}, u32[]{:S(2)}) copy-start(f32[32,7,512]{2,0,1:T(8,128)} %get-tuple-element.24) | copy-start | bytes 1376260
  205.1 31.2 %copy-start.8 = (f32[32,7,512]{2,0,1:T(8,128)S(1)}, f32[32,7,512]{2,0,1:T(8,128)}, u32[]{:S(2)}) copy-start(f32[32,7,512]{2,0,1:T(8,128)} %get-tuple-element.25) | copy-start | bytes 1376260
  206.1 26.3 %all-to-all-start.1 = ((f32[32,7,512]{2,1,0:T(8,128)}), f32[32,7,512]{2,1,0:T(8,128)S(1)}, u32[]{:S(2)}, u32[]{:S(2)}) async-start(f32[32,7,512]{2,1,0:T(8,128)} %copy.45), calls=%async_computation.1 | async-start | bytes 1048576 | tf_op jit(solution)/shard_map/all_to_all | solution.py:61
  232.4 21.5 %all-to-all-start.4 = ((f32[32,7,512]{2,1,0:T(8,128)}), f32[32,7,512]{2,1,0:T(8,128)S(1)}, u32[]{:S(2)}, u32[]{:S(2)}) async-start(f32[32,7,512]{2,1,0:T(8,128)} %copy.51), calls=%async_computation.4 | async-start | bytes 1048576 | tf_op jit(solution)/shard_map/all_to_all | solution.py:61
  254.0 21.9 %all-to-all-start.3 = ((f32[32,7,512]{2,1,0:T(8,128)}), f32[32,7,512]{2,1,0:T(8,128)S(1)}, u32[]{:S(2)}, u32[]{:S(2)}) async-start(f32[32,7,512]{2,1,0:T(8,128)} %copy.49), calls=%async_computation.3 | async-start | bytes 1048576 | tf_op jit(solution)/shard_map/all_to_all | solution.py:61
Sparse Core Ops, SparseCore 0:
  9.7 36.2 all-gather.8
  47.8 33.3 all-gather.10
  83.0 33.3 all-gather.6
  118.1 33.3 all-gather.4
where the time goes:
time: 310 us; the launch traced here: 309 us
  waiting for transfers between devices  160 us (52%)
  local copies, waits for them, and re-layouts  53.5 us (17%)
  starting transfers between devices  36.1 us (12%)
  matrix products  21.1 us (7%)
  blocking collectives  21 us (7%)
  between operations  13.5 us (4%)
  other arithmetic  3.49 us (1%)
    all_gather x4, waiting for transfers between devices, on_device(): lax.all_gather(integrals[:, c * w:(c + 1) * w], 'gy', axis=0, tiled=True)  67.5 us
    all_to_all x3, waiting for transfers between devices, on_device(): outs.append(lax.all_to_all(payload, 'pair', 0, 0, tiled=True))  50.7 us
    gather x4, local copies, waits for them, and re-layouts, pair_energies(): return jnp.take(energy, pairs[0]) + jnp.take(energy, pairs[1])  30.3 us
    all_to_all x1, waiting for transfers between devices, on_device(): t_all = lax.all_to_all(spread, 'pair', 0, 0, tiled=True)  28.6 us
    dot_general x4, matrix products, on_device(): jnp.dot(lhs, piece, precision=lax.Precision.HIGHEST, preferred_element_ty...  21.1 us
    all_to_all x1, blocking collectives, on_device(): outs.append(lax.all_to_all(payload, 'pair', 0, 0, tiled=True))  21 us
    all_to_all x3, starting transfers between devices, on_device(): outs.append(lax.all_to_all(payload, 'pair', 0, 0, tiled=True))  16.5 us
    all_to_all x1, starting transfers between devices, on_device(): t_all = lax.all_to_all(spread, 'pair', 0, 0, tiled=True)  10.2 us
  transfers between devices with their start and end apart: 13, of which 11 were waited for; matrix products, arithmetic and copies ran while one was open for 18% of the time, Pallas kernels for 0%

commit v1 on v0

--- a/solution.py
+++ b/solution.py
@@ -49,7 +49,13 @@
     w = columns // N_CHUNK
     outs = []
     for c in range(N_CHUNK):
-        piece = lax.all_gather(integrals[:, c * w : (c + 1) * w], "gy", axis=0, tiled=True)
+        here_x = integrals[:, c * w : (c + 1) * w]
+        piece = jnp.concatenate(
+            lax.all_to_all(
+                jnp.stack(tuple((here_x for _ in range(lax.axis_size("gy"))))), "gy", 0, 0
+            ),
+            axis=0,
+        )
         part = jnp.dot(
             lhs, piece, precision=lax.Precision.HIGHEST, preferred_element_type=jnp.float32
         )

time: 310 us -> 320 us (1.032)
  blocking collectives: 21 us -> 51.7 us
  waiting for transfers between devices: 160 us -> 141 us
  between operations: 13.5 us -> 0.47 us
  starting transfers between devices: 36.1 us -> 44.9 us
  local copies, waits for them, and re-layouts: 53.5 us -> 59.3 us
  matrix products: 21.1 us -> 17.8 us
    all_gather x4 -> x0, waiting for transfers between devices: 67.5 us -> none  [on_device(): lax.all_gather(integrals[:, c * w:(c + 1) * w], 'gy', axis=0, tiled=True)]
    all_to_all x0 -> x3, waiting for transfers between devices: none -> 48.7 us  [on_device(): lax.all_to_all(jnp.stack(tuple((here_x for _ in range(lax.axis_size('gy')...]
    all_to_all x0 -> x1, blocking collectives: none -> 30.7 us  [on_device(): lax.all_to_all(jnp.stack(tuple((here_x for _ in range(lax.axis_size('gy')...]
    all_to_all x0 -> x3, starting transfers between devices: none -> 11.9 us  [on_device(): lax.all_to_all(jnp.stack(tuple((here_x for _ in range(lax.axis_size('gy')...]
    all_to_all x1, waiting for transfers between devices: 28.6 us -> 39.9 us  [on_device(): t_all = lax.all_to_all(spread, 'pair', 0, 0, tiled=True)]
    ppermute x4, waiting for transfers between devices: 9.67 us -> 0.01 us  [on_device(): work = keep + lax.ppermute(send, 'gx', swap)]
    another operation x0 -> x4, local copies, waits for them, and re-layouts: none -> 5.08 us  [on_device(): jnp.stack(tuple((here_x for _ in range(lax.axis_size('gy')))))]
    all_to_all x3, starting transfers between devices: 16.5 us -> 12.8 us  [on_device(): outs.append(lax.all_to_all(payload, 'pair', 0, 0, tiled=True))]
  transfers between devices with their start and end apart: 13 -> 12, of which waited for: 11 -> 8; matrix products, arithmetic and copies ran while one was open for 18% -> 18% of each run, Pallas kernels for 0% -> 0%
where the time goes in v1:
time: 320 us; the launch traced here: 319 us
  waiting for transfers between devices  141 us (44%)
  local copies, waits for them, and re-layouts  59.3 us (19%)
  blocking collectives  51.7 us (16%)
  starting transfers between devices  44.9 us (14%)
  matrix products  17.8 us (6%)
  other arithmetic  3.47 us (1%)
    all_to_all x3, waiting for transfers between devices, on_device(): outs.append(lax.all_to_all(payload, 'pair', 0, 0, tiled=True))  50.8 us
    all_to_all x3, waiting for transfers between devices, on_device(): lax.all_to_all(jnp.stack(tuple((here_x for _ in range(lax.axis_size('gy')...  48.7 us
    all_to_all x1, waiting for transfers between devices, on_device(): t_all = lax.all_to_all(spread, 'pair', 0, 0, tiled=True)  39.9 us
    all_to_all x1, blocking collectives, on_device(): lax.all_to_all(jnp.stack(tuple((here_x for _ in range(lax.axis_size('gy')...  30.7 us
    gather x4, local copies, waits for them, and re-layouts, pair_energies(): return jnp.take(energy, pairs[0]) + jnp.take(energy, pairs[1])  30.1 us
    all_to_all x1, blocking collectives, on_device(): outs.append(lax.all_to_all(payload, 'pair', 0, 0, tiled=True))  21 us
    dot_general x4, matrix products, on_device(): jnp.dot(lhs, piece, precision=lax.Precision.HIGHEST, preferred_element_ty...  17.8 us
    all_to_all x3, starting transfers between devices, on_device(): outs.append(lax.all_to_all(payload, 'pair', 0, 0, tiled=True))  12.8 us
  transfers between devices with their start and end apart: 12, of which 8 were waited for; matrix products, arithmetic and copies ran while one was open for 18% of the time, Pallas kernels for 0%

profile of v1, /device:TPU:2, one launch (start us, length us, event | category | flops | bytes accessed | tf_op | source)
XLA Modules:
  0.0 319.0 jit_solution(14531354503891401753)
XLA Ops:
  0.0 1.7 fusion.16
  1.7 0.3 stack.61
  2.0 30.7 %all_to_all.45 = f32[4,256,512]{2,1,0:T(8,128)} all-to-all(f32[4,256,512]{2,1,0:T(8,128)S(1)} %stack.61), channel_id=1, replica_groups=mesh['pair'=32,'gy'=4,'gx'=2] {'gy'}, dimensions={0} | all-to-all | bytes 4194304 | tf_op jit(solution)/shard_map/all_to_all | solution.py:54
  32.7 1.6 stack.63
  34.3 3.7 %all-to-all-start.5 = ((f32[4,256,512]{2,1,0:T(8,128)}), f32[4,256,512]{2,1,0:T(8,128)S(1)}, u32[]{:S(2)}, u32[]{:S(2)}) async-start(f32[4,256,512]{2,1,0:T(8,128)} %stack.63), calls=%async_computation.5 | async-start | bytes 4194304 | tf_op jit(solution)/shard_map/all_to_all | solution.py:54
  38.1 25.4 %all-to-all-done.5 = f32[4,256,512]{2,1,0:T(8,128)S(1)} async-done(((f32[4,256,512]{2,1,0:T(8,128)}), f32[4,256,512]{2,1,0:T(8,128)S(1)}, u32[]{:S(2)}, u32[]{:S(2)}) %all-to-all-start.5) | async-done | bytes 2097184 | tf_op jit(solution)/shard_map/all_to_all | solution.py:54
  63.5 1.3 copy-done.3
  64.8 1.6 stack.65
  66.4 3.7 %all-to-all-start.7 = ((f32[4,256,512]{2,1,0:T(8,128)}), f32[4,256,512]{2,1,0:T(8,128)S(1)}, u32[]{:S(2)}, u32[]{:S(2)}) async-start(f32[4,256,512]{2,1,0:T(8,128)} %stack.65), calls=%async_computation.7 | async-start | bytes 4194304 | tf_op jit(solution)/shard_map/all_to_all | solution.py:54
  70.2 0.6 gather_fusion.2
  70.9 0.6 gather_fusion.3
  71.5 0.1 select_bitcast_fusion
  71.5 2.2 collective-permute-start
  73.7 0.6 gather_fusion
  74.4 0.6 gather_fusion.1
  75.0 0.1 select_bitcast_fusion.1
  75.1 2.0 collective-permute-done
  77.1 17.7 %all-to-all-done.7 = f32[4,256,512]{2,1,0:T(8,128)S(1)} async-done(((f32[4,256,512]{2,1,0:T(8,128)}), f32[4,256,512]{2,1,0:T(8,128)S(1)}, u32[]{:S(2)}, u32[]{:S(2)}) %all-to-all-start.7) | async-done | bytes 2097184 | tf_op jit(solution)/shard_map/all_to_all | solution.py:54
  94.8 1.4 copy-done.5
  96.2 1.7 broadcast_in_dim.34
  97.9 10.2 %all-to-all-start = ((f32[32,2,7,1024]{3,1,2,0:T(2,128)}), f32[32,2,7,1024]{3,1,2,0:T(2,128)S(1)}, u32[]{:S(2)}, u32[]{:S(2)}) async-start(f32[32,2,7,1024]{3,1,2,0:T(2,128)} %broadcast_in_dim.34), calls=%async_computation | async-start | bytes 3670016 | tf_op jit(solution)/shard_map/all_to_all | solution.py:44
  108.2 1.9 gather_fusion.4
  110.0 1.9 gather_fusion.5
  111.9 0.9 constant_dynamic-slice_fusion
  112.8 39.9 %all-to-all-done = f32[32,2,7,1024]{3,1,2,0:T(2,128)S(1)} async-done(((f32[32,2,7,1024]{3,1,2,0:T(2,128)}), f32[32,2,7,1024]{3,1,2,0:T(2,128)S(1)}, u32[]{:S(2)}, u32[]{:S(2)}) %all-to-all-start) | async-done | bytes 1835040 | tf_op jit(solution)/shard_map/all_to_all | solution.py:44
  152.8 1.6 stack.59
  154.3 4.4 %all-to-all-start.1 = ((f32[4,256,512]{2,1,0:T(8,128)}), f32[4,256,512]{2,1,0:T(8,128)}, u32[]{:S(2)}, u32[]{:S(2)}) async-start(f32[4,256,512]{2,1,0:T(8,128)} %stack.59), calls=%async_computation.1 | async-start | bytes 4194304 | tf_op jit(solution)/shard_map/all_to_all | solution.py:54
  158.8 5.3 %fusion.4 = f32[32,2,7,512]{3,0,2,1:T(8,128)S(1)} fusion(f32[1024,512,1,1]{1,0,3,2:T(8,128)} %bitcast.69, f32[32,2,7,1024]{3,1,2,0:T(2,128)S(1)} %all-to-all-done), kind=kOutput, calls=%fused_computation.13 | convolution fusion | flops 2818572288 | bytes 4849664 | tf_op jit(solution)/shard_map/dot_general | solution.py:59
  164.2 0.9 dynamic-slice_bitcast_fusion.2
  165.1 2.1 collective-permute-start.2
  167.2 3.6 %fusion.2 = f32[32,2,7,512]{3,0,2,1:T(8,128)S(1)} fusion(f32[1024,512,1,1]{1,0,3,2:T(8,128)S(1)} %bitcast.68, f32[32,2,7,1024]{3,1,2,0:T(2,128)S(1)} %all-to-all-done), kind=kOutput, calls=%fused_computation.11 | convolution fusion | flops 2818572288 | bytes 4849664 | tf_op jit(solution)/shard_map/dot_general | solution.py:59
  170.8 1.0 dynamic-slice_bitcast_fusion.1
  171.8 1.4 collective-permute-start.3
  173.2 3.6 %fusion = f32[32,2,7,512]{3,0,2,1:T(8,128)S(1)} fusion(f32[1024,512,1,1]{1,0,3,2:T(8,128)S(1)} %bitcast.70, f32[32,2,7,1024]{3,1,2,0:T(2,128)S(1)} %all-to-all-done), kind=kOutput, calls=%fused_computation.9 | convolution fusion | flops 2818572288 | bytes 4849664 | tf_op jit(solution)/shard_map/dot_general | solution.py:59
  176.8 0.9 dynamic-slice_bitcast_fusion
  177.8 0.2 copy-done.9
  177.9 2.1 collective-permute-start.4
  180.1 5.6 %all-to-all-done.1 = f32[4,256,512]{2,1,0:T(8,128)} async-done(((f32[4,256,512]{2,1,0:T(8,128)}), f32[4,256,512]{2,1,0:T(8,128)}, u32[]{:S(2)}, u32[]{:S(2)}) %all-to-all-start.1) | async-done | bytes 2097184 | tf_op jit(solution)/shard_map/all_to_all | solution.py:54
  185.7 5.2 %fusion.6 = f32[32,2,7,512]{3,0,2,1:T(8,128)S(1)} fusion(f32[1024,512,1,1]{1,0,3,2:T(8,128)} %bitcast.9, f32[32,2,7,1024]{3,1,2,0:T(2,128)S(1)} %all-to-all-done), kind=kOutput, calls=%fused_computation.15 | convolution fusion | flops 2818572288 | bytes 4849664 | tf_op jit(solution)/shard_map/dot_general | solution.py:59
  190.9 0.0 copy-start.11
  190.9 0.9 copy-done.11
  191.8 0.8 dynamic-slice_bitcast_fusion.3
  192.6 2.1 collective-permute-start.1
  194.8 13.2 %gather_fusion.6 = f32[2048]{0:T(1024)S(1)} fusion(f32[512]{0:T(512)S(1)} %copy-done, s32[2048]{0:T(1024)S(1)} %fusion.12), kind=kCustom, calls=%fused_computation.3.clone | custom fusion | bytes 24576 | tf_op jit(solution)/shard_map/jit(_take)/gather | solution.py:11
  208.0 13.2 %gather_fusion.7 = f32[2048]{0:T(1024)S(1)} fusion(f32[512]{0:T(512)S(1)} %copy-done, s32[2048]{0:T(1024)S(1)} %fusion.13), kind=kCustom, calls=%fused_computation.7.clone | custom fusion | bytes 24576 | tf_op jit(solution)/shard_map/jit(_take)/gather | solution.py:11
  221.2 0.1 sub.31
  221.3 0.1 copy.44
  221.4 0.0 collective-permute-done.4
  221.4 0.8 copy-done.14
  222.2 2.9 fusion.11
  225.2 1.1 copy.45
  226.3 4.6 %all-to-all-start.2 = ((f32[32,7,512]{2,1,0:T(8,128)}), f32[32,7,512]{2,1,0:T(8,128)S(1)}, u32[]{:S(2)}, u32[]{:S(2)}) async-start(f32[32,7,512]{2,1,0:T(8,128)} %copy.45), calls=%async_computation.2 | async-start | bytes 1048576 | tf_op jit(solution)/shard_map/all_to_all | solution.py:67
  230.8 1.1 copy.47
  231.9 16.7 %all-to-all-done.2 = f32[32,7,512]{2,1,0:T(8,128)S(1)} async-done(((f32[32,7,512]{2,1,0:T(8,128)}), f32[32,7,512]{2,1,0:T(8,128)S(1)}, u32[]{:S(2)}, u32[]{:S(2)}) %all-to-all-start.2) | async-done | bytes 458784 | tf_op jit(solution)/shard_map/all_to_all | solution.py:67
  248.6 4.1 %all-to-all-start.4 = ((f32[32,7,512]{2,1,0:T(8,128)}), f32[32,7,512]{2,1,0:T(8,128)S(1)}, u32[]{:S(2)}, u32[]{:S(2)}) async-start(f32[32,7,512]{2,1,0:T(8,128)} %copy.47), calls=%async_computation.4 | async-start | bytes 1048576 | tf_op jit(solution)/shard_map/all_to_all | solution.py:67
  252.7 1.1 copy.49
  253.8 16.7 %all-to-all-done.4 = f32[32,7,512]{2,1,0:T(8,128)S(1)} async-done(((f32[32,7,512]{2,1,0:T(8,128)}), f32[32,7,512]{2,1,0:T(8,128)S(1)}, u32[]{:S(2)}, u32[]{:S(2)}) %all-to-all-start.4) | async-done | bytes 458784 | tf_op jit(solution)/shard_map/all_to_all | solution.py:67
  270.5 4.1 %all-to-all-start.6 = ((f32[32,7,512]{2,1,0:T(8,128)}), f32[32,7,512]{2,1,0:T(8,128)S(1)}, u32[]{:S(2)}, u32[]{:S(2)}) async-start(f32[32,7,512]{2,1,0:T(8,128)} %copy.49), calls=%async_computation.6 | async-start | bytes 1048576 | tf_op jit(solution)/shard_map/all_to_all | solution.py:67
  274.6 0.3 copy.51
  274.9 17.5 %all-to-all-done.6 = f32[32,7,512]{2,1,0:T(8,128)S(1)} async-done(((f32[32,7,512]{2,1,0:T(8,128)}), f32[32,7,512]{2,1,0:T(8,128)S(1)}, u32[]{:S(2)}, u32[]{:S(2)}) %all-to-all-start.6) | async-done | bytes 458784 | tf_op jit(solution)/shard_map/all_to_all | solution.py:67
  292.4 21.0 %all_to_all.46 = f32[32,7,512]{2,1,0:T(8,128)S(1)} all-to-all(f32[32,7,512]{2,1,0:T(8,128)S(1)} %copy.51), channel_id=1, replica_groups=mesh['pair'=32,'gy'=4,'gx'=2] {'pair'}, dimensions={0} | all-to-all | bytes 917504 | tf_op jit(solution)/shard_map/all_to_all | solution.py:67
  313.3 0.3 maximum_bitcast_fusion
  313.6 1.2 copy.52
  314.8 4.2 %reshape.199 = f32[1,7,65536]{2,0,1:T(1,128)} reshape(f32[7,32,4,512]{3,2,1,0:T(4,128)S(1)} %copy.52) | data formatting | bytes 3670016 | tf_op jit(solution)/shard_map/reshape | solution.py:69
  (50 shorter events, 0.3 us)
Async XLA Ops:
  0.0 194.8 %copy-start = (f32[512]{0:T(512)S(1)}, f32[512]{0:T(512)}, u32[]{:S(2)}) copy-start(f32[512]{0:T(512)} %param.21) | copy-start | bytes 6148
  34.3 3.8 %copy-start.15 = (f32[1,7,2048]{2,0,1:T(1,128)S(1)}, f32[1,7,2048]{2,0,1:T(1,128)}, u32[]{:S(2)}) copy-start(f32[1,7,2048]{2,0,1:T(1,128)} %param.15) | copy-start | bytes 172036
  34.3 29.2 %all-to-all-start.5 = ((f32[4,256,512]{2,1,0:T(8,128)}), f32[4,256,512]{2,1,0:T(8,128)S(1)}, u32[]{:S(2)}, u32[]{:S(2)}) async-start(f32[4,256,512]{2,1,0:T(8,128)} %stack.63), calls=%async_computation.5 | async-start | bytes 4194304 | tf_op jit(solution)/shard_map/all_to_all | solution.py:54
  63.5 1.3 copy-start.3
  66.4 3.8 %copy-start.2 = (s32[16]{0:T(128)S(1)}, s32[16]{0:T(128)}, u32[]{:S(2)}) copy-start(s32[16]{0:T(128)} %param.17) | copy-start | bytes 196
  66.4 28.3 %all-to-all-start.7 = ((f32[4,256,512]{2,1,0:T(8,128)}), f32[4,256,512]{2,1,0:T(8,128)S(1)}, u32[]{:S(2)}, u32[]{:S(2)}) async-start(f32[4,256,512]{2,1,0:T(8,128)} %stack.65), calls=%async_computation.7 | async-start | bytes 4194304 | tf_op jit(solution)/shard_map/all_to_all | solution.py:54
  71.5 5.5 %collective-permute-start = (f32[7,1024]{1,0:T(8,128)S(1)}, f32[7,1024]{1,0:T(8,128)S(1)}, u32[]{:S(2)}, u32[]{:S(2)}) collective-permute-start(f32[7,1024]{1,0:T(8,128)S(1)} %select_bitcast_fusion), channel_id=1, source_target_pairs={{0,1},{1,0},{2,3},{3,2},{4,5},{5,4},{6,7},{7,6},{8,9},{9,8},{10,11... | collective-permute-start | bytes 86024 | tf_op jit(solution)/shard_map/ppermute | solution.py:41
  94.8 1.4 copy-start.5
  97.9 10.2 %copy-start.16 = (s32[1,2,224]{2,1,0:T(2,128)S(1)}, s32[1,2,224]{2,1,0:T(2,128)}, u32[]{:S(2)}) copy-start(s32[1,2,224]{2,1,0:T(2,128)} %param.18) | copy-start | bytes 5380
  97.9 10.3 %copy-start.1 = (f32[64]{0:T(128)S(1)}, f32[64]{0:T(128)}, u32[]{:S(2)}) copy-start(f32[64]{0:T(128)} %param.20) | copy-start | bytes 772
  97.9 54.9 %all-to-all-start = ((f32[32,2,7,1024]{3,1,2,0:T(2,128)}), f32[32,2,7,1024]{3,1,2,0:T(2,128)S(1)}, u32[]{:S(2)}, u32[]{:S(2)}) async-start(f32[32,2,7,1024]{3,1,2,0:T(2,128)} %broadcast_in_dim.34), calls=%async_computation | async-start | bytes 3670016 | tf_op jit(solution)/shard_map/all_to_all | solution.py:44
  154.3 31.3 %all-to-all-start.1 = ((f32[4,256,512]{2,1,0:T(8,128)}), f32[4,256,512]{2,1,0:T(8,128)}, u32[]{:S(2)}, u32[]{:S(2)}) async-start(f32[4,256,512]{2,1,0:T(8,128)} %stack.59), calls=%async_computation.1 | async-start | bytes 4194304 | tf_op jit(solution)/shard_map/all_to_all | solution.py:54
  158.8 8.4 %copy-start.4 = (f32[4,256,512]{2,1,0:T(8,128)S(1)}, f32[4,256,512]{2,1,0:T(8,128)}, u32[]{:S(2)}) copy-start(f32[4,256,512]{2,1,0:T(8,128)} %copy-done.3) | copy-start | bytes 6291460
  165.1 56.3 %collective-permute-start.2 = (f32[32,7,512]{2,0,1:T(8,128)}, f32[32,7,512]{2,0,1:T(8,128)S(1)}, u32[]{:S(2)}, u32[]{:S(2)}) collective-permute-start(f32[32,7,512]{2,0,1:T(8,128)} %dynamic-slice_bitcast_fusion.2), channel_id=1, source_target_pairs={{0,1},{1,0},{2,3},{3,2},{4,5},{5,4},{6,7},{7,6},{8,9},{9,8},{10,11... | collective-permute-start | bytes 1376264 | tf_op jit(solution)/shard_map/ppermute | solution.py:65
  167.2 6.0 %copy-start.6 = (f32[4,256,512]{2,1,0:T(8,128)S(1)}, f32[4,256,512]{2,1,0:T(8,128)}, u32[]{:S(2)}) copy-start(f32[4,256,512]{2,1,0:T(8,128)} %copy-done.5) | copy-start | bytes 6291460
  170.8 6.0 %copy-start.7 = (f32[32,2,7,512]{3,0,2,1:T(8,128)}, f32[32,2,7,512]{3,0,2,1:T(8,128)S(1)}, u32[]{:S(2)}) copy-start(f32[32,2,7,512]{3,0,2,1:T(8,128)S(1)} %fusion.2) | copy-start | bytes 2752516
  171.8 49.6 %collective-permute-start.3 = (f32[32,7,512]{2,0,1:T(8,128)}, f32[32,7,512]{2,0,1:T(8,128)}, u32[]{:S(2)}, u32[]{:S(2)}) collective-permute-start(f32[32,7,512]{2,0,1:T(8,128)} %dynamic-slice_bitcast_fusion.1), channel_id=1, source_target_pairs={{0,1},{1,0},{2,3},{3,2},{4,5},{5,4},{6,7},{7,6},{8,9},{9,8},{10,11... | collective-permute-start | bytes 1376264 | tf_op jit(solution)/shard_map/ppermute | solution.py:65
  176.8 1.1 copy-start.9
  177.9 43.5 %collective-permute-start.4 = (f32[32,7,512]{2,0,1:T(8,128)}, f32[32,7,512]{2,0,1:T(8,128)}, u32[]{:S(2)}, u32[]{:S(2)}) collective-permute-start(f32[32,7,512]{2,0,1:T(8,128)} %dynamic-slice_bitcast_fusion), channel_id=1, source_target_pairs={{0,1},{1,0},{2,3},{3,2},{4,5},{5,4},{6,7},{7,6},{8,9},{9,8},{10,11... | collective-permute-start | bytes 1376264 | tf_op jit(solution)/shard_map/ppermute | solution.py:65
  190.9 0.9 copy-start.11
  192.6 28.8 %collective-permute-start.1 = (f32[32,7,512]{2,0,1:T(8,128)}, f32[32,7,512]{2,0,1:T(8,128)}, u32[]{:S(2)}, u32[]{:S(2)}) collective-permute-start(f32[32,7,512]{2,0,1:T(8,128)} %dynamic-slice_bitcast_fusion.3), channel_id=1, source_target_pairs={{0,1},{1,0},{2,3},{3,2},{4,5},{5,4},{6,7},{7,6},{8,9},{9,8},{10,11... | collective-permute-start | bytes 1376264 | tf_op jit(solution)/shard_map/ppermute | solution.py:65
  208.0 14.3 %copy-start.8 = (f32[32,2,7,512]{3,0,2,1:T(8,128)S(1)}, f32[32,2,7,512]{3,0,2,1:T(8,128)}, u32[]{:S(2)}) copy-start(f32[32,2,7,512]{3,0,2,1:T(8,128)} %copy-done.7) | copy-start | bytes 2752516
  208.0 14.3 %copy-start.10 = (f32[32,2,7,512]{3,0,2,1:T(8,128)S(1)}, f32[32,2,7,512]{3,0,2,1:T(8,128)}, u32[]{:S(2)}) copy-start(f32[32,2,7,512]{3,0,2,1:T(8,128)} %copy-done.9) | copy-start | bytes 2752516
  221.4 0.8 copy-start.14
  225.2 5.6 %copy-start.13 = (f32[32,7,512]{2,0,1:T(8,128)S(1)}, f32[32,7,512]{2,0,1:T(8,128)}, u32[]{:S(2)}) copy-start(f32[32,7,512]{2,0,1:T(8,128)} %get-tuple-element.26) | copy-start | bytes 1376260
  225.2 27.5 %copy-start.12 = (f32[32,7,512]{2,0,1:T(8,128)S(1)}, f32[32,7,512]{2,0,1:T(8,128)}, u32[]{:S(2)}) copy-start(f32[32,7,512]{2,0,1:T(8,128)} %get-tuple-element.25) | copy-start | bytes 1376260
  226.3 22.3 %all-to-all-start.2 = ((f32[32,7,512]{2,1,0:T(8,128)}), f32[32,7,512]{2,1,0:T(8,128)S(1)}, u32[]{:S(2)}, u32[]{:S(2)}) async-start(f32[32,7,512]{2,1,0:T(8,128)} %copy.45), calls=%async_computation.2 | async-start | bytes 1048576 | tf_op jit(solution)/shard_map/all_to_all | solution.py:67
  248.6 21.9 %all-to-all-start.4 = ((f32[32,7,512]{2,1,0:T(8,128)}), f32[32,7,512]{2,1,0:T(8,128)S(1)}, u32[]{:S(2)}, u32[]{:S(2)}) async-start(f32[32,7,512]{2,1,0:T(8,128)} %copy.47), calls=%async_computation.4 | async-start | bytes 1048576 | tf_op jit(solution)/shard_map/all_to_all | solution.py:67
  270.5 21.9 %all-to-all-start.6 = ((f32[32,7,512]{2,1,0:T(8,128)}), f32[32,7,512]{2,1,0:T(8,128)S(1)}, u32[]{:S(2)}, u32[]{:S(2)}) async-start(f32[32,7,512]{2,1,0:T(8,128)} %copy.49), calls=%async_computation.6 | async-start | bytes 1048576 | tf_op jit(solution)/shard_map/all_to_all | solution.py:67
